TPU v7x, 128 devices: a whole 4x4x4 slice. The times are simulated.
128 devices in a mesh: ang: 64 (over x, y_lo, z, core), pix: 2 (over y_hi).
Axes of the slice: x: 4, y: 4 (y_hi: 2, y_lo: 2; y = y_hi * 2 + y_lo), z: 4, core: 2. Of those that a mesh axis runs over, the one named last changes fastest.
Arguments:
- grads: bfloat16 [2, 4096, 128, 512], P(None, 'ang', 'pix')
- circle_pos: int32 [4096], replicated, may hold values from 0 to 4095, as said below
- harmonics: int32 [256], replicated, may hold values from 0 to 4095, as said below
- support: int32 [128, 512], replicated, may hold values 0 or 1
Outputs:
- update: bfloat16 [2, 4096, 128, 512], P(None, 'ang', 'pix')
- harmonic_rms: float32 [256], replicated
Inputs may be any that keep to these rules, and one draw needn't show every extreme that they name: `circle_pos`: the stored angles form 64 aligned blocks of 64 rows; block b holds the circle positions r_b + 64 * j for j = 0 to 63 in this order, and the 64 values r_b are distinct. `harmonics`: 256 distinct harmonic numbers, among them 0 and 4095.
All inputs are finite; a program needn't handle non-finite values.
Results may differ from a plain program's by a relative error of at most 0.015.
Values may be sent and summed in bfloat16 or wider, within the bound.
No kernel may reach another device: no remote copies, remote signals or barrier semaphores. Data moves between devices by JAX's collectives and lax.ppermute only.
A program may use at most 192 MiB of HBM per device.

v0:
```python
import math
import jax
import jax.numpy as jnp
from jax import lax
from jax.sharding import PartitionSpec as P


def phase_pair(product, modulus):
    radians = (product % modulus).astype(jnp.float32) * (2.0 * math.pi / modulus)
    return (jnp.cos(radians), jnp.sin(radians))


def split_parts(value):
    if value.dtype == jnp.bfloat16:
        return (value,)
    high = value.astype(jnp.bfloat16)
    low = (value - high.astype(jnp.float32)).astype(jnp.bfloat16)
    return (high, low)


def split_einsum(form, left, right):
    left_parts = split_parts(left)
    right_parts = split_parts(right)
    total = None
    for left_rank, left_piece in enumerate(left_parts):
        for right_rank, right_piece in enumerate(right_parts):
            if left_rank + right_rank <= 1:
                term = jnp.einsum(form, left_piece, right_piece, preferred_element_type=jnp.float32)
                total = term if total is None else total + term
    return total


def normalize(coef_re, coef_im, weight, cell_count):
    square_sums = jnp.sum(weight[None, :] * (coef_re * coef_re + coef_im * coef_im), axis=1)
    totals = lax.psum(square_sums, ("ang", "pix"))
    harmonic_rms = jnp.sqrt(totals / cell_count + 1e-06)
    factor = weight[None, :] / harmonic_rms[:, None]
    return (coef_re * factor, coef_im * factor, harmonic_rms)


def direct_path(grads, circle_pos, harmonics, weight, cell_count):
    angle_count = circle_pos.shape[0]
    kept_count = harmonics.shape[0]
    moved = lax.all_to_all(grads, "ang", split_axis=2, concat_axis=1, tiled=True)
    row_local = moved.shape[2]
    col_count = moved.shape[3]
    flat = moved.reshape(2, angle_count, row_local * col_count)
    pixel_count = flat.shape[2]
    phase_cos, phase_sin = phase_pair(harmonics[:, None] * circle_pos[None, :], angle_count)
    table = jnp.concatenate((phase_cos, phase_sin), 0)
    products = split_einsum("ka,ap->kp", table, jnp.concatenate((flat[0], flat[1]), 1))
    scale = 1.0 / math.sqrt(angle_count)
    coef_re = (products[:kept_count, :pixel_count] + products[kept_count:, pixel_count:]) * scale
    coef_im = (products[:kept_count, pixel_count:] - products[kept_count:, :pixel_count]) * scale
    step_re, step_im, harmonic_rms = normalize(coef_re, coef_im, weight, cell_count)
    right_side = jnp.concatenate(
        (jnp.concatenate((step_re, -step_im), 0), jnp.concatenate((step_im, step_re), 0)), 1
    )
    synthesis = split_einsum("ka,kp->ap", table, right_side)
    scale_back = 1.0 / math.sqrt(kept_count)
    update = jnp.stack((synthesis[:, :pixel_count], synthesis[:, pixel_count:])) * scale_back
    update = update.astype(jnp.bfloat16).reshape(2, angle_count, row_local, col_count)
    return (lax.all_to_all(update, "ang", split_axis=1, concat_axis=2, tiled=True), harmonic_rms)


def body(grads, circle_pos, harmonics, support):
    ang_count = lax.axis_size("ang")
    row_pix = grads.shape[2]
    row_local = row_pix // ang_count
    col_count = grads.shape[3]
    row_start = lax.axis_index("pix") * row_pix + lax.axis_index("ang") * row_local
    weight = (
        lax.dynamic_slice_in_dim(support, row_start, row_local, 0).astype(jnp.float32).reshape(-1)
    )
    cell_count = float(row_pix * lax.axis_size("pix") * col_count)
    update, harmonic_rms = direct_path(grads, circle_pos, harmonics, weight, cell_count)
    return (update, harmonic_rms)


def solution(mesh):
    placed = (P(None, "ang", "pix", None), P(), P(), P())
    return jax.shard_map(
        body,
        mesh=mesh,
        in_specs=placed,
        out_specs=(P(None, "ang", "pix", None), P()),
        check_vma=False,
    )
```

profile of v0, /device:TPU:1, one launch (start us, length us, event | category | flops | bytes accessed | tf_op | source)
XLA Modules:
  0.0 437.9 jit_solution(5942899219189294290)
XLA Ops:
  0.6 11.5 %copy.18 = bf16[2,64,64,512]{3,1,0,2:T(8,128)(2,1)} copy(bf16[2,64,64,512]{3,2,1,0:T(8,128)(2,1)} %param.4) | data formatting | bytes 16777216 | tf_op args[0]
  12.1 11.2 %all-to-all-start = ((bf16[2,64,64,512]{3,1,0,2:T(8,128)(2,1)}), bf16[2,64,64,512]{3,1,0,2:T(8,128)(2,1)}, u32[]{:S(2)}, u32[]{:S(2)}) async-start(bf16[2,64,64,512]{3,1,0,2:T(8,128)(2,1)} %copy.18), calls=%async_computation | async-start | bytes 16777216 | tf_op jit(solution)/shard_map/all_to_all | solution.py:44
  23.3 0.7 dynamic-slice_convert_fusion
  24.1 18.0 %fusion.8 = (f32[256,4096]{1,0:T(8,128)}, f32[256,4096]{1,0:T(8,128)}) fusion(s32[4096]{0:T(1024)S(1)} %copy-done.6, s32[256]{0:T(256)S(1)} %copy-done.8), kind=kLoop, calls=%fused_computation.23 | loop fusion | flops 14680064 | bytes 8406016 | tf_op jit(solution)/shard_map/cos | solution.py:10
  42.1 84.6 %all-to-all-done = bf16[2,64,64,512]{3,1,0,2:T(8,128)(2,1)} async-done(((bf16[2,64,64,512]{3,1,0,2:T(8,128)(2,1)}), bf16[2,64,64,512]{3,1,0,2:T(8,128)(2,1)}, u32[]{:S(2)}, u32[]{:S(2)}) %all-to-all-start) | async-done | bytes 8388640 | tf_op jit(solution)/shard_map/all_to_all | solution.py:44
  126.7 7.9 %copy.24 = bf16[2,64,64,512]{3,1,2,0:T(8,128)(2,1)} copy(bf16[2,64,64,512]{3,1,0,2:T(8,128)(2,1)} %all-to-all-done) | data formatting | bytes 16777216 | tf_op jit(solution)/shard_map/all_to_all | solution.py:44
  134.6 5.4 %fusion.27 = (bf16[1,64,64,1,512]{4,2,1,3,0:T(8,128)(2,1)S(1)}, bf16[1,64,64,1,512]{4,2,1,3,0:T(8,128)(2,1)}) fusion(bf16[2,64,64,1,512]{4,2,1,3,0:T(8,128)(2,1)} %bitcast.17), kind=kLoop, calls=%fused_computation.41 | loop fusion | bytes 16777216 | tf_op jit(solution)/shard_map/slice | solution.py:51
  140.0 2.1 copy-done.5
  142.1 1.5 copy-done.2
  143.6 8.0 %fusion.2 = f32[512,1024]{1,0:T(8,128)} fusion(bf16[4096,512]{1,0:T(8,128)(2,1)} %bitcast.21, bf16[4096,512]{1,0:T(8,128)(2,1)S(1)} %bitcast.19, f32[256,4096]{1,0:T(8,128)S(1)} %copy-done.2, f32[256,4096]{1,0:T(8,128)S(1)} %copy-done), kind=kOutput, calls=%fused_computation.15 | convolution fusion | flops 4322230272 | bytes 18874368 | tf_op jit(solution)/shard_map/ka,ap->kp/dot_general | solution.py:28
  151.6 8.5 %fusion.9 = f32[512,1024]{1,0:T(8,128)S(1)} fusion(f32[512,1024]{1,0:T(8,128)} %fusion.2, bf16[4096,512]{1,0:T(8,128)(2,1)} %bitcast.22, bf16[4096,512]{1,0:T(8,128)(2,1)} %bitcast.20, f32[256,4096]{1,0:T(8,128)S(1)} %copy-done.2, f32[256,4096]{1,0:T(8,128)S(1)} %copy-done), kind=kOutput, calls=%fused_computation.24 | convolution fusion | flops 4320657408 | bytes 20971520 | tf_op jit(solution)/shard_map/ka,ap->kp/dot_general | solution.py:28
  160.2 1.3 copy-done.4
  161.5 0.2 multiply_reduce_fusion
  161.7 70.5 %psum.7 = f32[256]{0:T(256)S(1)} all-reduce(f32[256]{0:T(256)S(1)} %multiply_reduce_fusion), channel_id=1, replica_groups=mesh['ang'=64,'pix'=2] {'ang','pix'}, use_global_device_ids=true, to_apply=%region_1.2 | all-reduce | flops 256 | bytes 2048 | tf_op jit(solution)/shard_map/psum | solution.py:35
  232.3 1.7 fusion.26
  234.0 12.7 %fusion.11 = f32[4096,1024]{1,0:T(8,128)} fusion(f32[256,512]{1,0:T(8,128)S(1)} %get-tuple-element.12, f32[256,512]{1,0:T(8,128)S(1)} %get-tuple-element.7, f32[256,512]{1,0:T(8,128)S(1)} %get-tuple-element.6, f32[256,4096]{1,0:T(8,128)} %get-tuple-element.14, f32[256,4096]{1,0:T(8,128)} %get-tuple-element.13), kind=kOutput, calls=%fused_computation.26 | convolution fusion | flops 4307025920 | bytes 26738688 | tf_op jit(solution)/shard_map/ka,kp->ap/dot_general | solution.py:28
  246.7 8.2 %fusion.19 = f32[4096,1024]{1,0:T(8,128)} fusion(f32[256,512]{1,0:T(8,128)S(1)} %get-tuple-element.12, f32[256,512]{1,0:T(8,128)S(1)} %get-tuple-element.7, f32[256,512]{1,0:T(8,128)S(1)} %get-tuple-element.6, f32[256,4096]{1,0:T(8,128)S(1)} %copy-done.3, f32[256,4096]{1,0:T(8,128)S(1)} %copy-done.1), kind=kOutput, calls=%fused_computation.39 | convolution fusion | flops 4307550208 | bytes 26738688 | tf_op jit(solution)/shard_map/ka,kp->ap/dot_general | solution.py:28
  254.9 19.3 %add_add_fusion = f32[4096,1024]{1,0:T(8,128)} fusion(f32[4096,1024]{1,0:T(8,128)} %fusion.19, f32[4096,1024]{1,0:T(8,128)} %fusion.11, f32[256,512]{1,0:T(8,128)S(1)} %get-tuple-element.12, f32[256,512]{1,0:T(8,128)S(1)} %get-tuple-element.7, f32[256,512]{1,0:T(8,128)S(1)} %get-tuple-element.6, f32[256,4096]{1,0:T(8,128)} %get-tuple-element.14, ...), kind=kOutput, calls=%fused_computation.2 | convolution fusion | flops 4318035968 | bytes 60293120 | tf_op jit(solution)/shard_map/ka,kp->ap/dot_general | solution.py:28
  274.1 6.9 %slice_bitcast_fusion.1 = (f32[1,4096,1,512]{3,1,2,0:T(8,128)S(1)}, f32[1,4096,1,512]{3,1,2,0:T(8,128)S(1)}) fusion(f32[4096,1024]{1,0:T(8,128)} %add_add_fusion), kind=kLoop, calls=%fused_computation.4 | loop fusion | bytes 33554432 | tf_op jit(solution)/shard_map/stack | solution.py:61
  281.0 2.5 fusion
  283.5 32.6 %copy.20 = bf16[2,4096,1,512]{3,0,2,1:T(2,128)(2,1)S(1)} copy(bf16[2,4096,1,512]{3,1,2,0:T(8,128)(2,1)S(1)} %fusion) | data formatting | bytes 16777216 | tf_op jit(solution)/shard_map/convert_element_type | solution.py:62
  316.2 102.3 %all_to_all.33 = bf16[2,4096,1,512]{3,0,2,1:T(2,128)(2,1)} all-to-all(bf16[2,4096,1,512]{3,0,2,1:T(2,128)(2,1)S(1)} %copy.20), channel_id=1, replica_groups=mesh['ang'=64,'pix'=2] {'ang'}, dimensions={1} | all-to-all | bytes 16777216 | tf_op jit(solution)/shard_map/all_to_all | solution.py:63
  418.4 8.0 %copy.21 = bf16[2,4096,1,512]{3,1,0,2:T(8,128)(2,1)} copy(bf16[2,4096,1,512]{3,0,2,1:T(2,128)(2,1)} %all_to_all.33) | data formatting | bytes 16777216 | tf_op jit(solution)/shard_map/all_to_all | solution.py:63
  426.4 11.5 %copy.22 = bf16[2,64,64,512]{3,2,1,0:T(8,128)(2,1)} copy(bf16[2,64,64,512]{3,1,2,0:T(8,128)(2,1)} %bitcast.18) | data formatting | bytes 16777216
  (16 shorter events, 0.0 us)
Async XLA Ops:
  12.1 11.9 %copy-start.6 = (s32[4096]{0:T(1024)S(1)}, s32[4096]{0:T(1024)}, u32[]{:S(2)}) copy-start(s32[4096]{0:T(1024)} %param.5) | copy-start | bytes 49156
  12.1 11.9 %copy-start.8 = (s32[256]{0:T(256)S(1)}, s32[256]{0:T(256)}, u32[]{:S(2)}) copy-start(s32[256]{0:T(256)} %param.6) | copy-start | bytes 3076
  12.1 114.6 %all-to-all-start = ((bf16[2,64,64,512]{3,1,0,2:T(8,128)(2,1)}), bf16[2,64,64,512]{3,1,0,2:T(8,128)(2,1)}, u32[]{:S(2)}, u32[]{:S(2)}) async-start(bf16[2,64,64,512]{3,1,0,2:T(8,128)(2,1)} %copy.18), calls=%async_computation | async-start | bytes 16777216 | tf_op jit(solution)/shard_map/all_to_all | solution.py:44
  134.6 7.5 %copy-start = (f32[256,4096]{1,0:T(8,128)S(1)}, f32[256,4096]{1,0:T(8,128)}, u32[]{:S(2)}) copy-start(f32[256,4096]{1,0:T(8,128)} %get-tuple-element.13) | copy-start | bytes 12582916
  134.6 9.0 %copy-start.2 = (f32[256,4096]{1,0:T(8,128)S(1)}, f32[256,4096]{1,0:T(8,128)}, u32[]{:S(2)}) copy-start(f32[256,4096]{1,0:T(8,128)} %get-tuple-element.14) | copy-start | bytes 12582916
  140.0 2.1 copy-start.5
  160.1 1.3 copy-start.4
  232.2 14.4 %copy-start.7 = (f32[256]{0:T(256)}, f32[256]{0:T(256)S(1)}, u32[]{:S(2)}) copy-start(f32[256]{0:T(256)S(1)} %add_sqrt_fusion) | copy-start | bytes 3076
  234.0 12.7 %copy-start.1 = (f32[256,4096]{1,0:T(8,128)S(1)}, f32[256,4096]{1,0:T(8,128)}, u32[]{:S(2)}) copy-start(f32[256,4096]{1,0:T(8,128)} %get-tuple-element.13) | copy-start | bytes 12582916
  234.0 12.7 %copy-start.3 = (f32[256,4096]{1,0:T(8,128)S(1)}, f32[256,4096]{1,0:T(8,128)}, u32[]{:S(2)}) copy-start(f32[256,4096]{1,0:T(8,128)} %get-tuple-element.14) | copy-start | bytes 12582916
where the time goes:
time: 438 us
  blocking collectives  173 us (39%)
  local copies, waits for them, and re-layouts  88.7 us (20%)
  waiting for transfers between devices  84.6 us (19%)
  matrix products  56.7 us (13%)
  other arithmetic  23.2 us (5%)
  starting transfers between devices  11.2 us (3%)
    all_to_all x1, blocking collectives, direct_path(): lax.all_to_all(update, 'ang', split_axis=1, concat_axis=2, tiled=True)  102 us
    all_to_all x1, waiting for transfers between devices, direct_path(): lax.all_to_all(grads, 'ang', split_axis=2, concat_axis=1, tiled=True)  84.6 us
    psum x1, blocking collectives, normalize(): totals = lax.psum(square_sums, ('ang', 'pix'))  70.5 us
    dot_general x5, matrix products, split_einsum(): jnp.einsum(form, left_piece, right_piece, preferred_element_type=jnp.floa...  56.7 us
    convert_element_type x1, local copies, waits for them, and re-layouts, direct_path(): update.astype(jnp.bfloat16).reshape(2, angle_count, row_local, col_count)  32.6 us
    unnamed x20, local copies, waits for them, and re-layouts  28 us
    cos x1, other arithmetic, phase_pair(): return (jnp.cos(radians), jnp.sin(radians))  18 us
    all_to_all x1, starting transfers between devices, direct_path(): lax.all_to_all(grads, 'ang', split_axis=2, concat_axis=1, tiled=True)  11.2 us
  transfers between devices with their start and end apart: 1, of which 1 were waited for; matrix products, arithmetic and copies ran while one was open for 4% of the time, Pallas kernels for 0%

commit v1 on v0

--- a/solution.py
+++ b/solution.py
@@ -3,6 +3,15 @@
 import jax.numpy as jnp
 from jax import lax
 from jax.sharding import PartitionSpec as P
+
+
+def lead_fields(target, out_dim, k_dim):
+    v1 = lax.axis_size("ang")
+    current_block = jnp.split(target, v1, out_dim)
+    p_next = jnp.stack(current_block, 0)
+    small = lax.all_to_all(p_next, axis_name="ang", split_axis=0, concat_axis=0)
+    piece_now = jnp.concatenate(small, k_dim)
+    return piece_now
 
 
 def phase_pair(product, modulus):
@@ -60,7 +69,7 @@
     scale_back = 1.0 / math.sqrt(kept_count)
     update = jnp.stack((synthesis[:, :pixel_count], synthesis[:, pixel_count:])) * scale_back
     update = update.astype(jnp.bfloat16).reshape(2, angle_count, row_local, col_count)
-    return (lax.all_to_all(update, "ang", split_axis=1, concat_axis=2, tiled=True), harmonic_rms)
+    return (lead_fields(update, 1, 2), harmonic_rms)
 
 
 def body(grads, circle_pos, harmonics, support):

time: 438 us -> 402 us (0.918)
  local copies, waits for them, and re-layouts: 88.7 us -> 48.8 us
    convert_element_type x1 -> x0, local copies, waits for them, and re-layouts: 32.6 us -> none  [direct_path(): update.astype(jnp.bfloat16).reshape(2, angle_count, row_local, col_count)]
    all_to_all x1 -> x0, local copies, waits for them, and re-layouts: 7.96 us -> none  [direct_path(): lax.all_to_all(update, 'ang', split_axis=1, concat_axis=2, tiled=True)]
    unnamed x20 -> x83, local copies, waits for them, and re-layouts: 28 us -> 28.7 us
  transfers between devices with their start and end apart: 1 -> 1, of which waited for: 1 -> 1; matrix products, arithmetic and copies ran while one was open for 4% -> 5% of each run, Pallas kernels for 0% -> 0%
where the time goes in v1:
time: 402 us; the launch traced here: 401 us
  blocking collectives  173 us (43%)
  waiting for transfers between devices  84.6 us (21%)
  matrix products  56.7 us (14%)
  local copies, waits for them, and re-layouts  48.8 us (12%)
  other arithmetic  25.7 us (6%)
  starting transfers between devices  11.2 us (3%)
    all_to_all x1, blocking collectives, lead_fields(): small = lax.all_to_all(p_next, axis_name='ang', split_axis=0, concat_axis=0)  102 us
    all_to_all x1, waiting for transfers between devices, direct_path(): lax.all_to_all(grads, 'ang', split_axis=2, concat_axis=1, tiled=True)  84.6 us
    psum x1, blocking collectives, normalize(): totals = lax.psum(square_sums, ('ang', 'pix'))  70.5 us
    dot_general x5, matrix products, split_einsum(): jnp.einsum(form, left_piece, right_piece, preferred_element_type=jnp.floa...  56.7 us
    unnamed x83, local copies, waits for them, and re-layouts  28.7 us
    cos x1, other arithmetic, phase_pair(): return (jnp.cos(radians), jnp.sin(radians))  18 us
    all_to_all x1, starting transfers between devices, direct_path(): lax.all_to_all(grads, 'ang', split_axis=2, concat_axis=1, tiled=True)  11.2 us
  transfers between devices with their start and end apart: 1, of which 1 were waited for; matrix products, arithmetic and copies ran while one was open for 5% of the time, Pallas kernels for 0%

profile of v1, /device:TPU:1, one launch (start us, length us, event | category | flops | bytes accessed | tf_op | source)
XLA Modules:
  0.0 401.0 jit_solution(6046276937413356461)
XLA Ops:
  0.6 11.5 %copy.135 = bf16[2,64,64,512]{3,1,0,2:T(8,128)(2,1)} copy(bf16[2,64,64,512]{3,2,1,0:T(8,128)(2,1)} %param.4) | data formatting | bytes 16777216 | tf_op args[0]
  12.1 11.2 %all-to-all-start = ((bf16[2,64,64,512]{3,1,0,2:T(8,128)(2,1)}), bf16[2,64,64,512]{3,1,0,2:T(8,128)(2,1)}, u32[]{:S(2)}, u32[]{:S(2)}) async-start(bf16[2,64,64,512]{3,1,0,2:T(8,128)(2,1)} %copy.135), calls=%async_computation | async-start | bytes 16777216 | tf_op jit(solution)/shard_map/all_to_all | solution.py:53
  23.3 0.7 dynamic-slice_convert_fusion
  24.1 18.0 %fusion.8 = (f32[256,4096]{1,0:T(8,128)}, f32[256,4096]{1,0:T(8,128)}) fusion(s32[4096]{0:T(1024)S(1)} %copy-done.6, s32[256]{0:T(256)S(1)} %copy-done.8), kind=kLoop, calls=%fused_computation.23 | loop fusion | flops 14680064 | bytes 8406016 | tf_op jit(solution)/shard_map/cos | solution.py:19
  42.1 84.6 %all-to-all-done = bf16[2,64,64,512]{3,1,0,2:T(8,128)(2,1)} async-done(((bf16[2,64,64,512]{3,1,0,2:T(8,128)(2,1)}), bf16[2,64,64,512]{3,1,0,2:T(8,128)(2,1)}, u32[]{:S(2)}, u32[]{:S(2)}) %all-to-all-start) | async-done | bytes 8388640 | tf_op jit(solution)/shard_map/all_to_all | solution.py:53
  126.7 7.9 %copy.202 = bf16[2,64,64,512]{3,1,2,0:T(8,128)(2,1)} copy(bf16[2,64,64,512]{3,1,0,2:T(8,128)(2,1)} %all-to-all-done) | data formatting | bytes 16777216 | tf_op jit(solution)/shard_map/all_to_all | solution.py:53
  134.6 5.4 %fusion.27 = (bf16[1,64,64,1,512]{4,2,1,3,0:T(8,128)(2,1)S(1)}, bf16[1,64,64,1,512]{4,2,1,3,0:T(8,128)(2,1)}) fusion(bf16[2,64,64,1,512]{4,2,1,3,0:T(8,128)(2,1)} %bitcast.335), kind=kLoop, calls=%fused_computation.169 | loop fusion | bytes 16777216 | tf_op jit(solution)/shard_map/slice | solution.py:60
  140.0 2.1 copy-done.5
  142.1 1.5 copy-done.2
  143.6 8.0 %fusion.2 = f32[512,1024]{1,0:T(8,128)} fusion(bf16[4096,512]{1,0:T(8,128)(2,1)} %bitcast.339, bf16[4096,512]{1,0:T(8,128)(2,1)S(1)} %bitcast.337, f32[256,4096]{1,0:T(8,128)S(1)} %copy-done.2, f32[256,4096]{1,0:T(8,128)S(1)} %copy-done), kind=kOutput, calls=%fused_computation.15 | convolution fusion | flops 4322230272 | bytes 18874368 | tf_op jit(solution)/shard_map/ka,ap->kp/dot_general | solution.py:37
  151.6 8.5 %fusion.9 = f32[512,1024]{1,0:T(8,128)S(1)} fusion(f32[512,1024]{1,0:T(8,128)} %fusion.2, bf16[4096,512]{1,0:T(8,128)(2,1)} %bitcast.340, bf16[4096,512]{1,0:T(8,128)(2,1)} %bitcast.338, f32[256,4096]{1,0:T(8,128)S(1)} %copy-done.2, f32[256,4096]{1,0:T(8,128)S(1)} %copy-done), kind=kOutput, calls=%fused_computation.24 | convolution fusion | flops 4320657408 | bytes 20971520 | tf_op jit(solution)/shard_map/ka,ap->kp/dot_general | solution.py:37
  160.1 0.0 copy-start.4
  160.2 1.3 copy-done.4
  161.5 0.2 multiply_reduce_fusion
  161.7 70.5 %psum.7 = f32[256]{0:T(256)S(1)} all-reduce(f32[256]{0:T(256)S(1)} %multiply_reduce_fusion), channel_id=1, replica_groups=mesh['ang'=64,'pix'=2] {'ang','pix'}, use_global_device_ids=true, to_apply=%region_1.2 | all-reduce | flops 256 | bytes 2048 | tf_op jit(solution)/shard_map/psum | solution.py:44
  232.3 1.7 fusion.26
  234.0 12.7 %fusion.11 = f32[4096,1024]{1,0:T(8,128)} fusion(f32[256,512]{1,0:T(8,128)S(1)} %get-tuple-element.14, f32[256,512]{1,0:T(8,128)S(1)} %get-tuple-element.9, f32[256,512]{1,0:T(8,128)S(1)} %get-tuple-element.8, f32[256,4096]{1,0:T(8,128)} %get-tuple-element.16, f32[256,4096]{1,0:T(8,128)} %get-tuple-element.15), kind=kOutput, calls=%fused_computation.26 | convolution fusion | flops 4307025920 | bytes 26738688 | tf_op jit(solution)/shard_map/ka,kp->ap/dot_general | solution.py:37
  246.7 8.2 %fusion.19 = f32[4096,1024]{1,0:T(8,128)} fusion(f32[256,512]{1,0:T(8,128)S(1)} %get-tuple-element.14, f32[256,512]{1,0:T(8,128)S(1)} %get-tuple-element.9, f32[256,512]{1,0:T(8,128)S(1)} %get-tuple-element.8, f32[256,4096]{1,0:T(8,128)S(1)} %copy-done.3, f32[256,4096]{1,0:T(8,128)S(1)} %copy-done.1), kind=kOutput, calls=%fused_computation.167 | convolution fusion | flops 4307550208 | bytes 26738688 | tf_op jit(solution)/shard_map/ka,kp->ap/dot_general | solution.py:37
  254.9 19.3 %add_add_fusion = f32[4096,1024]{1,0:T(8,128)} fusion(f32[4096,1024]{1,0:T(8,128)} %fusion.19, f32[4096,1024]{1,0:T(8,128)} %fusion.11, f32[256,512]{1,0:T(8,128)S(1)} %get-tuple-element.14, f32[256,512]{1,0:T(8,128)S(1)} %get-tuple-element.9, f32[256,512]{1,0:T(8,128)S(1)} %get-tuple-element.8, f32[256,4096]{1,0:T(8,128)} %get-tuple-element.16, ...), kind=kOutput, calls=%fused_computation.2 | convolution fusion | flops 4318035968 | bytes 60293120 | tf_op jit(solution)/shard_map/ka,kp->ap/dot_general | solution.py:37
  274.1 6.9 %slice_bitcast_fusion.1 = (f32[1,4096,1,512]{3,1,2,0:T(8,128)S(1)}, f32[1,4096,1,512]{3,1,2,0:T(8,128)S(1)}) fusion(f32[4096,1024]{1,0:T(8,128)} %add_add_fusion), kind=kLoop, calls=%fused_computation.4 | loop fusion | bytes 33554432 | tf_op jit(solution)/shard_map/stack | solution.py:70
  281.0 2.5 fusion.28
  283.5 2.5 fusion
  287.3 102.3 %all_to_all.20 = bf16[64,2,64,1,512]{4,2,1,3,0:T(8,128)(2,1)} all-to-all(bf16[64,2,64,1,512]{4,2,1,3,0:T(8,128)(2,1)S(1)} %constant_dynamic-update-slice_fusion), channel_id=1, replica_groups=mesh['ang'=64,'pix'=2] {'ang'}, dimensions={0} | all-to-all | bytes 16777216 | tf_op jit(solution)/shard_map/all_to_all | solution.py:12
  389.5 11.5 %copy.200 = bf16[2,64,64,512]{3,2,1,0:T(8,128)(2,1)} copy(bf16[2,64,64,512]{3,1,0,2:T(8,128)(2,1)} %bitcast.336) | data formatting | bytes 16777216
  (79 shorter events, 0.7 us)
Async XLA Ops:
  12.1 11.9 %copy-start.6 = (s32[4096]{0:T(1024)S(1)}, s32[4096]{0:T(1024)}, u32[]{:S(2)}) copy-start(s32[4096]{0:T(1024)} %param.5) | copy-start | bytes 49156
  12.1 11.9 %copy-start.8 = (s32[256]{0:T(256)S(1)}, s32[256]{0:T(256)}, u32[]{:S(2)}) copy-start(s32[256]{0:T(256)} %param.6) | copy-start | bytes 3076
  12.1 114.6 %all-to-all-start = ((bf16[2,64,64,512]{3,1,0,2:T(8,128)(2,1)}), bf16[2,64,64,512]{3,1,0,2:T(8,128)(2,1)}, u32[]{:S(2)}, u32[]{:S(2)}) async-start(bf16[2,64,64,512]{3,1,0,2:T(8,128)(2,1)} %copy.135), calls=%async_computation | async-start | bytes 16777216 | tf_op jit(solution)/shard_map/all_to_all | solution.py:53
  134.6 7.5 %copy-start = (f32[256,4096]{1,0:T(8,128)S(1)}, f32[256,4096]{1,0:T(8,128)}, u32[]{:S(2)}) copy-start(f32[256,4096]{1,0:T(8,128)} %get-tuple-element.15) | copy-start | bytes 12582916
  134.6 9.0 %copy-start.2 = (f32[256,4096]{1,0:T(8,128)S(1)}, f32[256,4096]{1,0:T(8,128)}, u32[]{:S(2)}) copy-start(f32[256,4096]{1,0:T(8,128)} %get-tuple-element.16) | copy-start | bytes 12582916
  140.0 2.1 copy-start.5
  160.1 1.3 copy-start.4
  232.2 14.4 %copy-start.7 = (f32[256]{0:T(256)}, f32[256]{0:T(256)S(1)}, u32[]{:S(2)}) copy-start(f32[256]{0:T(256)S(1)} %add_sqrt_fusion) | copy-start | bytes 3076
  234.0 12.7 %copy-start.1 = (f32[256,4096]{1,0:T(8,128)S(1)}, f32[256,4096]{1,0:T(8,128)}, u32[]{:S(2)}) copy-start(f32[256,4096]{1,0:T(8,128)} %get-tuple-element.15) | copy-start | bytes 12582916
  234.0 12.7 %copy-start.3 = (f32[256,4096]{1,0:T(8,128)S(1)}, f32[256,4096]{1,0:T(8,128)}, u32[]{:S(2)}) copy-start(f32[256,4096]{1,0:T(8,128)} %get-tuple-element.16) | copy-start | bytes 12582916
